TPU v7x, 256 devices: a whole 4x4x8 slice. The times are simulated.
256 devices in a mesh: hyp: 32 (over y, x, core), head: 8 (over z).
Axes of the slice: x: 4, y: 4, z: 8, core: 2. Of those that a mesh axis runs over, the one named last changes fastest.
Arguments:
- step_embeds: bfloat16 [3, 512, 4096], P(None, 'hyp'), may hold values from -6 to 6
- lang_table: bfloat16 [8, 4096], replicated, may hold values from -3 to 3
- lang_ids: int32 [32, 4], replicated, may hold values from 0 to 7
- self_gain: float32 [4096], replicated, may hold values from 0.1 to 1.9
- self_wq: bfloat16 [4096, 2048], P(None, 'head'), may hold values from -0.09375 to 0.09375
- self_wk: bfloat16 [4096, 2048], P(None, 'head'), may hold values from -0.09375 to 0.09375
- self_wv: bfloat16 [4096, 2048], P(None, 'head'), may hold values from -0.09375 to 0.09375
- self_wo: bfloat16 [2048, 4096], P('head'), may hold values from -0.125 to 0.125
- cross_gain: float32 [4096], replicated, may hold values from 0.1 to 1.9
- cross_wq: bfloat16 [4096, 2048], P(None, 'head'), may hold values from -0.09375 to 0.09375
- cross_wkv: bfloat16 [4096, 4096], P('hyp', 'head'), may hold values from -0.09375 to 0.09375
- encoder_rows: bfloat16 [24576, 4096], P('hyp', 'head'), may hold values from -200 to 200
- doc_lengths: int32 [32], P('hyp'), may hold values from 192 to 768, as said below
- past_keys: bfloat16 [512, 32, 2048], P('hyp', None, 'head'), may hold values from -200 to 200
- past_values: bfloat16 [512, 32, 2048], P('hyp', None, 'head'), may hold values from -6 to 6
- parents: int32 [3, 512], replicated, may hold values from 0 to 3
Outputs:
- cross_context: bfloat16 [3, 512, 2048], P(None, 'hyp', 'head')
- final_keys: bfloat16 [512, 35, 2048], P('hyp', None, 'head')
- final_values: bfloat16 [512, 35, 2048], P('hyp', None, 'head')
Inputs may be any that keep to these rules, and one draw needn't show every extreme that they name: `doc_lengths`: some document has exactly 768 live rows. `parents`: A parent is a beam of the same document and target.
All inputs are finite; a program needn't handle non-finite values.
Results may differ from a plain program's by a relative error of at most 0.03.
Values may be sent and summed in bfloat16 or wider, within the bound.
No kernel may reach another device: no remote copies, remote signals or barrier semaphores. Data moves between devices by JAX's collectives and lax.ppermute only.
A program may use at most 128 MiB of HBM per device.

v0:
```python
import jax
import jax.numpy as jnp
from jax import lax
from jax.sharding import PartitionSpec as P

HEAD = 256
BEAMS = 4
TARGETS = 4
STEPS = 3
EPSILON = 1e-06


def rms_scaled(values_in, gain):
    mean_square = jnp.mean(values_in * values_in, axis=-1, keepdims=True)
    return values_in * lax.rsqrt(mean_square + EPSILON) * gain


def pick_rows(candidates, selector, row_axis):
    shape_list = [1] * candidates[0].ndim
    shape_list[row_axis] = selector.shape[0]
    chosen = candidates[0]
    for position in range(1, len(candidates)):
        chosen = jnp.where((selector == position).reshape(shape_list), candidates[position], chosen)
    return chosen


def beam_copies(block, hyp_count, group_size):
    copies = [block]
    for hop in range(1, BEAMS):
        distance = hop * group_size
        route = [((i - distance) % hyp_count, i) for i in range(hyp_count)]
        copies.append(lax.ppermute(block, "hyp", route))
    return copies


def cross_attend(queries, cross_keys, cross_values, doc_length, scaling):
    scores = (
        jnp.einsum("qd,jd->qj", queries, cross_keys, preferred_element_type=jnp.float32) * scaling
    )
    live_mask = lax.broadcasted_iota(jnp.int32, (1, cross_keys.shape[0]), 1) < doc_length
    scores = jnp.where(live_mask, scores, -jnp.inf)
    highest = jnp.max(scores, axis=1, keepdims=True)
    raw_weights = jnp.exp(scores - highest)
    totals = jnp.sum(raw_weights, axis=1, keepdims=True)
    weights = (raw_weights / totals).astype(jnp.bfloat16)
    output = jnp.einsum("qj,jd->qd", weights, cross_values, preferred_element_type=jnp.float32)
    return output.astype(jnp.bfloat16)


def shards(
    step_embeds,
    lang_table,
    lang_ids,
    self_gain,
    self_wq,
    self_wk,
    self_wv,
    self_wo,
    cross_gain,
    cross_wq,
    cross_wkv,
    encoder_rows,
    doc_lengths,
    past_keys,
    past_values,
    parents,
):
    hyp_count = lax.axis_size("hyp")
    group_size = hyp_count // BEAMS
    my_index = lax.axis_index("hyp")
    my_beam = my_index // group_size
    my_slot = my_index % group_size
    steps = step_embeds.shape[0]
    row_count = step_embeds.shape[1]
    docs_here = row_count // TARGETS
    head_width = self_wq.shape[1]
    doc_count = lang_ids.shape[0]
    past_len = past_keys.shape[1]
    scaling = HEAD ** (-0.5)
    full_weights = lax.all_gather(cross_wkv, "hyp", axis=0, tiled=True)
    full_rows = lax.all_gather(encoder_rows, "head", axis=1, tiled=True)
    cross_kv = jnp.dot(full_rows, full_weights, preferred_element_type=jnp.float32).astype(
        jnp.bfloat16
    )
    cross_kv = cross_kv.reshape(encoder_rows.shape[0], 2, HEAD)
    cross_keys = cross_kv[:, 0, :]
    cross_values = cross_kv[:, 1, :]
    doc_length = doc_lengths[0]
    past_stack = jnp.stack([past_keys, past_values])
    past_all = beam_copies(past_stack, hyp_count, group_size)
    my_langs = lax.dynamic_slice_in_dim(lang_ids, my_slot * docs_here, docs_here, 0).reshape(
        row_count
    )
    one_hot = (
        my_langs[:, None] == lax.broadcasted_iota(jnp.int32, (1, lang_table.shape[0]), 1)
    ).astype(jnp.bfloat16)
    lang_rows = jnp.dot(one_hot, lang_table, preferred_element_type=jnp.float32)
    hidden_in = step_embeds.astype(jnp.float32) + lang_rows[None]
    normed = rms_scaled(hidden_in, self_gain).astype(jnp.bfloat16).reshape(steps * row_count, -1)
    new_query = jnp.dot(normed, self_wq, preferred_element_type=jnp.float32).astype(jnp.bfloat16)
    new_key = jnp.dot(normed, self_wk, preferred_element_type=jnp.float32).astype(jnp.bfloat16)
    new_value = jnp.dot(normed, self_wv, preferred_element_type=jnp.float32).astype(jnp.bfloat16)
    new_query = new_query.reshape(steps, row_count, head_width)
    fresh = jnp.stack([new_key, new_value]).reshape(2, steps, row_count, head_width)
    fresh_all = beam_copies(fresh, hyp_count, group_size)
    parent_view = parents.reshape(steps, BEAMS, doc_count * TARGETS)
    parent_of = lax.dynamic_slice_in_dim(parent_view, my_slot * row_count, row_count, 2)
    own_beam = jnp.full((row_count,), my_beam, jnp.int32)

    def hop_of(beam):
        return (my_beam - beam) % BEAMS

    def climb(step_idx, beam):
        return jnp.take_along_axis(parent_of[step_idx], beam[None, :], axis=0)[0]

    def cache_at(step_idx):
        ancestor = own_beam
        new_parts = [None] * (step_idx + 1)
        new_parts[step_idx] = fresh[:, step_idx]
        for back in range(step_idx, 0, -1):
            ancestor = climb(back, ancestor)
            new_parts[back - 1] = pick_rows(
                [f[:, back - 1] for f in fresh_all], hop_of(ancestor), 1
            )
        ancestor = climb(0, ancestor)
        past_part = pick_rows(past_all, hop_of(ancestor), 1)
        return jnp.concatenate([past_part] + [n[:, :, None, :] for n in new_parts], axis=2)

    contexts = []
    final_cache = None
    for step_idx in range(steps):
        cache = cache_at(step_idx)
        if step_idx == steps - 1:
            final_cache = cache
        query = new_query[step_idx]
        scores = (
            jnp.einsum("rd,rpd->rp", query, cache[0], preferred_element_type=jnp.float32) * scaling
        )
        highest = jnp.max(scores, axis=1, keepdims=True)
        raw_weights = jnp.exp(scores - highest)
        totals = jnp.sum(raw_weights, axis=1, keepdims=True)
        summed = jnp.einsum(
            "rp,rpd->rd",
            raw_weights,
            cache[1].astype(jnp.float32),
            preferred_element_type=jnp.float32,
        )
        contexts.append((summed / totals).astype(jnp.bfloat16))
    self_context = jnp.stack(contexts).reshape(steps * row_count, head_width)
    partial_out = jnp.dot(self_context, self_wo, preferred_element_type=jnp.float32)
    summed_out = lax.psum(partial_out.astype(jnp.bfloat16), "head").astype(jnp.float32)
    residual = hidden_in + summed_out.reshape(hidden_in.shape)
    normed_cross = rms_scaled(residual, cross_gain).astype(jnp.bfloat16)
    cross_query = jnp.dot(
        normed_cross.reshape(steps * row_count, -1), cross_wq, preferred_element_type=jnp.float32
    ).astype(jnp.bfloat16)
    by_doc = cross_query.reshape(steps, docs_here, TARGETS, head_width)
    sent = []
    for shift in range(BEAMS):
        route = [
            (beam * group_size + slot, slot * docs_here + (beam + shift) % BEAMS)
            for beam in range(BEAMS)
            for slot in range(group_size)
        ]
        piece = lax.dynamic_index_in_dim(by_doc, (my_beam + shift) % BEAMS, 1, keepdims=False)
        sent.append(lax.ppermute(piece, "hyp", route))
    doc_queries = jnp.stack(sent).reshape(BEAMS * steps * TARGETS, head_width)
    answer = cross_attend(doc_queries, cross_keys, cross_values, doc_length, scaling)
    answer = answer.reshape(BEAMS, steps, TARGETS, head_width)
    back = []
    for shift in range(BEAMS):
        route = [
            (slot * docs_here + (beam + shift) % BEAMS, beam * group_size + slot)
            for beam in range(BEAMS)
            for slot in range(group_size)
        ]
        back.append(lax.ppermute(answer[shift], "hyp", route))
    back = jnp.stack(back)
    order = (jnp.arange(docs_here, dtype=jnp.int32) - my_beam) % BEAMS
    by_k = jnp.take(back, order, axis=0)
    contexts_out = by_k.transpose(1, 0, 2, 3).reshape(steps, row_count, head_width)
    return (contexts_out, final_cache[0], final_cache[1])


def solution(mesh):
    return jax.shard_map(
        shards,
        mesh=mesh,
        in_specs=(
            P(None, "hyp", None),
            P(),
            P(),
            P(),
            P(None, "head"),
            P(None, "head"),
            P(None, "head"),
            P("head", None),
            P(),
            P(None, "head"),
            P("hyp", "head"),
            P("hyp", "head"),
            P("hyp"),
            P("hyp", None, "head"),
            P("hyp", None, "head"),
            P(),
        ),
        out_specs=(P(None, "hyp", "head"), P("hyp", None, "head"), P("hyp", None, "head")),
        check_vma=False,
    )
```

profile of v0, /device:TPU:17, one launch (start us, length us, event | category | flops | bytes accessed | tf_op | source)
XLA Modules:
  0.0 224.9 jit_solution(5241141596806689058)
XLA Ops:
  8.1 0.9 constant_dynamic-slice_fusion
  9.2 1.1 fusion.42
  10.2 1.3 multiply_reduce_fusion.1
  11.6 1.2 multiply_convert_fusion.1
  12.8 2.1 convolution_convert_fusion.4
  14.9 0.5 convolution_convert_fusion.5
  15.4 0.2 collective-permute-start.3
  15.6 2.6 %collective-permute-start.4 = (bf16[2,3,16,256]{3,2,0,1:T(8,128)(2,1)S(1)}, bf16[2,3,16,256]{3,2,0,1:T(8,128)(2,1)S(1)}, u32[]{:S(2)}, u32[]{:S(2)}) collective-permute-start(bf16[2,3,16,256]{3,2,0,1:T(8,128)(2,1)S(1)} %pad_maximum_fusion.4), channel_id=1, source_target_pairs={{128,0},{136,8},{144,16},{152,24},{160,32},{168,40},{176,48},{184,... | collective-permute-start | bytes 147464 | tf_op jit(solution)/shard_map/ppermute | solution.py:32
  18.3 0.3 copy_bitcast_fusion
  18.6 0.8 pad_maximum_fusion.2
  19.4 1.5 collective-permute-start
  20.9 1.6 collective-permute-start.1
  22.7 0.7 gather_fusion.4
  23.4 0.5 broadcast_compare_fusion.12
  23.9 0.7 gather_fusion.2
  24.6 0.5 copy-done.10
  25.1 1.2 gather_fusion.5
  26.3 0.7 fusion.61
  27.0 0.7 gather_fusion.1
  27.7 0.7 gather_fusion.3
  28.4 1.2 broadcast_compare_fusion.16
  29.6 0.5 broadcast_compare_fusion.9
  30.1 1.1 broadcast_compare_fusion.6
  31.2 0.7 gather_fusion.6
  32.0 2.1 convolution_convert_fusion.6
  34.2 0.3 collective-permute-start.2
  34.7 11.1 %collective-permute-done.2 = bf16[2,16,32,256]{3,1,2,0:T(8,128)(2,1)S(1)} collective-permute-done((bf16[2,16,32,256]{3,1,2,0:T(8,128)(2,1)}, bf16[2,16,32,256]{3,1,2,0:T(8,128)(2,1)S(1)}, u32[]{:S(2)}, u32[]{:S(2)}) %collective-permute-start.2) | collective-permute-done | bytes 524320 | tf_op jit(solution)/shard_map/ppermute | solution.py:32
  45.8 1.5 select_select_fusion.2
  47.5 0.2 fusion.3
  47.7 0.1 multiply_reduce_fusion.2
  47.8 0.2 fusion.66
  48.2 0.2 fusion.7
  48.4 0.1 multiply_reduce_fusion.3
  48.5 0.2 fusion.64
  48.7 0.2 fusion.11
  48.9 0.1 multiply_reduce_fusion.4
  49.1 0.2 fusion.63
  49.3 0.2 fusion.1
  49.6 0.2 fusion.5
  49.9 0.2 fusion.9
  50.2 1.2 convolution_convert_fusion
  51.6 0.5 all-gather.5.cloned.1.call-update
  52.1 0.5 all-gather.3.cloned.1.call-update
  53.4 78.1 %all-reduce.2.cloned.1.call-done = bf16[3,16,4096]{2,1,0:T(8,128)(2,1)} async-done(((bf16[3,16,4096]{2,1,0:T(8,128)(2,1)}), bf16[3,16,4096]{2,1,0:T(8,128)(2,1)}) %all-reduce.2.cloned.1.call-update) | async-done | bytes 393232 | tf_op jit(solution)/shard_map/psum | solution.py:151
  131.6 1.4 multiply_reduce_fusion
  133.0 1.2 multiply_convert_fusion
  134.2 0.5 convolution_convert_fusion.3
  134.7 4.6 %collective-permute-start.9 = (bf16[3,4,256]{2,1,0:T(4,128)(2,1)S(1)}, bf16[3,4,256]{2,1,0:T(4,128)(2,1)S(1)}, u32[]{:S(2)}, u32[]{:S(2)}) collective-permute-start(bf16[3,4,256]{2,1,0:T(4,128)(2,1)S(1)} %get-tuple-element.43), channel_id=1, source_target_pairs={{0,24},{8,56},{16,88},{24,120},{32,152},{40,184},{48,216},{56,248}... | collective-permute-start | bytes 18440 | tf_op jit(solution)/shard_map/ppermute | solution.py:166
  139.3 12.5 %collective-permute-start.8 = (bf16[3,4,256]{2,1,0:T(4,128)(2,1)S(1)}, bf16[3,4,256]{2,1,0:T(4,128)(2,1)S(1)}, u32[]{:S(2)}, u32[]{:S(2)}) collective-permute-start(bf16[3,4,256]{2,1,0:T(4,128)(2,1)S(1)} %get-tuple-element.44), channel_id=1, source_target_pairs={{0,16},{8,48},{16,80},{24,112},{32,144},{40,176},{48,208},{56,240}... | collective-permute-start | bytes 18440 | tf_op jit(solution)/shard_map/ppermute | solution.py:166
  151.8 5.5 %collective-permute-start.7 = (bf16[3,4,256]{2,1,0:T(4,128)(2,1)S(1)}, bf16[3,4,256]{2,1,0:T(4,128)(2,1)S(1)}, u32[]{:S(2)}, u32[]{:S(2)}) collective-permute-start(bf16[3,4,256]{2,1,0:T(4,128)(2,1)S(1)} %get-tuple-element.45), channel_id=1, source_target_pairs={{0,8},{8,40},{16,72},{24,104},{32,136},{40,168},{48,200},{56,232},... | collective-permute-start | bytes 18440 | tf_op jit(solution)/shard_map/ppermute | solution.py:166
  157.3 3.3 %collective-permute-start.6 = (bf16[3,4,256]{2,1,0:T(4,128)(2,1)S(1)}, bf16[3,4,256]{2,1,0:T(4,128)(2,1)S(1)}, u32[]{:S(2)}, u32[]{:S(2)}) collective-permute-start(bf16[3,4,256]{2,1,0:T(4,128)(2,1)S(1)} %get-tuple-element.42), channel_id=1, source_target_pairs={{0,0},{8,32},{16,64},{24,96},{32,128},{40,160},{48,192},{56,224},{... | collective-permute-start | bytes 18440 | tf_op jit(solution)/shard_map/ppermute | solution.py:166
  160.6 4.0 %collective-permute-done.6 = bf16[3,4,256]{2,1,0:T(4,128)(2,1)S(1)} collective-permute-done((bf16[3,4,256]{2,1,0:T(4,128)(2,1)S(1)}, bf16[3,4,256]{2,1,0:T(4,128)(2,1)S(1)}, u32[]{:S(2)}, u32[]{:S(2)}) %collective-permute-start.6) | collective-permute-done | bytes 6176 | tf_op jit(solution)/shard_map/ppermute | solution.py:166
  164.7 21.2 %all-gather.3.cloned.1.call-done = bf16[768,4096]{1,0:T(8,128)(2,1)} async-done(((bf16[768,512]{1,0:T(8,128)(2,1)}), bf16[768,4096]{1,0:T(8,128)(2,1)}) %all-gather.3.cloned.1.call-update) | async-done | bytes 6291472 | tf_op jit(solution)/shard_map/all_gather | solution.py:81
  186.0 7.5 %convolution_convert_fusion.1 = bf16[768,512]{0,1:T(8,128)(2,1)S(1)} fusion(bf16[768,4096]{1,0:T(8,128)(2,1)} %all-gather.3.cloned.1.call-done, bf16[4096,512]{1,0:T(8,128)(2,1)} %all-gather.5.cloned.1.call-done), kind=kOutput, calls=%fused_computation.8 | convolution fusion | flops 3221618688 | bytes 11272192 | tf_op jit(solution)/shard_map/dot_general | solution.py:82
  193.4 0.3 fusion.68
  193.7 0.2 fusion.16
  193.9 0.2 convolution_convert_fusion.2
  194.3 5.6 %collective-permute-start.13 = (bf16[3,4,256]{2,1,0:T(4,128)(2,1)S(1)}, bf16[3,4,256]{2,1,0:T(4,128)(2,1)S(1)}, u32[]{:S(2)}, u32[]{:S(2)}) collective-permute-start(bf16[3,4,256]{2,1,0:T(4,128)(2,1)S(1)} %squeeze.124), channel_id=1, source_target_pairs={{24,0},{56,8},{88,16},{120,24},{152,32},{184,40},{216,48},{248,56}... | collective-permute-start | bytes 18440 | tf_op jit(solution)/shard_map/ppermute | solution.py:177
  199.9 1.7 collective-permute-start.12
  201.7 5.9 %collective-permute-start.11 = (bf16[3,4,256]{2,1,0:T(4,128)(2,1)S(1)}, bf16[3,4,256]{2,1,0:T(4,128)(2,1)S(1)}, u32[]{:S(2)}, u32[]{:S(2)}) collective-permute-start(bf16[3,4,256]{2,1,0:T(4,128)(2,1)S(1)} %squeeze.122), channel_id=1, source_target_pairs={{8,0},{40,8},{72,16},{104,24},{136,32},{168,40},{200,48},{232,56},... | collective-permute-start | bytes 18440 | tf_op jit(solution)/shard_map/ppermute | solution.py:177
  207.6 2.9 %collective-permute-start.10 = (bf16[3,4,256]{2,1,0:T(4,128)(2,1)S(1)}, bf16[3,4,256]{2,1,0:T(4,128)(2,1)S(1)}, u32[]{:S(2)}, u32[]{:S(2)}) collective-permute-start(bf16[3,4,256]{2,1,0:T(4,128)(2,1)S(1)} %squeeze.121), channel_id=1, source_target_pairs={{0,0},{32,8},{64,16},{96,24},{128,32},{160,40},{192,48},{224,56},{... | collective-permute-start | bytes 18440 | tf_op jit(solution)/shard_map/ppermute | solution.py:177
  210.6 5.6 %collective-permute-done.10 = bf16[3,4,256]{2,1,0:T(4,128)(2,1)S(1)} collective-permute-done((bf16[3,4,256]{2,1,0:T(4,128)(2,1)S(1)}, bf16[3,4,256]{2,1,0:T(4,128)(2,1)S(1)}, u32[]{:S(2)}, u32[]{:S(2)}) %collective-permute-start.10) | collective-permute-done | bytes 6176 | tf_op jit(solution)/shard_map/ppermute | solution.py:177
  216.2 0.6 gather_fusion
  216.9 0.6 reshape.460
  (100 shorter events, 2.0 us)
Async XLA Ops:
  8.0 42.2 %copy-start = (bf16[256,4096]{1,0:T(8,128)(2,1)S(1)}, bf16[256,4096]{1,0:T(8,128)(2,1)}, u32[]{:S(2)}) copy-start(bf16[256,4096]{1,0:T(8,128)(2,1)} %param.25) | copy-start | bytes 6291460
  8.0 123.5 %all-reduce.2.cloned.1.call-start = ((), (), s32[]{:S(2)}) async-start(), calls=%async_computation | async-start | bytes 786432 | tf_op jit(solution)/shard_map/psum | solution.py:151
  10.2 4.7 %copy-start.2 = (bf16[4096,256]{1,0:T(8,128)(2,1)S(1)}, bf16[4096,256]{1,0:T(8,128)(2,1)}, u32[]{:S(2)}) copy-start(bf16[4096,256]{1,0:T(8,128)(2,1)} %param.23) | copy-start | bytes 6291460
  12.7 5.5 %copy-start.6 = (bf16[16,32,256]{2,1,0:T(8,128)(2,1)S(1)}, bf16[16,32,256]{2,1,0:T(8,128)(2,1)}, u32[]{:S(2)}) copy-start(bf16[16,32,256]{2,1,0:T(8,128)(2,1)} %param.32) | copy-start | bytes 786436
  12.7 5.5 %copy-start.7 = (bf16[16,32,256]{2,1,0:T(8,128)(2,1)S(1)}, bf16[16,32,256]{2,1,0:T(8,128)(2,1)}, u32[]{:S(2)}) copy-start(bf16[16,32,256]{2,1,0:T(8,128)(2,1)} %param.31) | copy-start | bytes 786436
  14.9 7.5 %copy-start.9 = (s32[3,512]{1,0:T(4,128)S(1)}, s32[3,512]{1,0:T(4,128)}, u32[]{:S(2)}) copy-start(s32[3,512]{1,0:T(4,128)} %param.33) | copy-start | bytes 18436
  15.4 18.8 %collective-permute-start.3 = (bf16[2,3,16,256]{3,2,0,1:T(8,128)(2,1)S(1)}, bf16[2,3,16,256]{3,2,0,1:T(8,128)(2,1)S(1)}, u32[]{:S(2)}, u32[]{:S(2)}) collective-permute-start(bf16[2,3,16,256]{3,2,0,1:T(8,128)(2,1)S(1)} %pad_maximum_fusion.4), channel_id=1, source_target_pairs={{64,0},{72,8},{80,16},{88,24},{96,32},{104,40},{112,48},{120,56},{... | collective-permute-start | bytes 147464 | tf_op jit(solution)/shard_map/ppermute | solution.py:32
  15.6 18.8 %collective-permute-start.4 = (bf16[2,3,16,256]{3,2,0,1:T(8,128)(2,1)S(1)}, bf16[2,3,16,256]{3,2,0,1:T(8,128)(2,1)S(1)}, u32[]{:S(2)}, u32[]{:S(2)}) collective-permute-start(bf16[2,3,16,256]{3,2,0,1:T(8,128)(2,1)S(1)} %pad_maximum_fusion.4), channel_id=1, source_target_pairs={{128,0},{136,8},{144,16},{152,24},{160,32},{168,40},{176,48},{184,... | collective-permute-start | bytes 147464 | tf_op jit(solution)/shard_map/ppermute | solution.py:32
  18.3 16.2 %collective-permute-start.5 = (bf16[2,3,16,256]{3,2,0,1:T(8,128)(2,1)S(1)}, bf16[2,3,16,256]{3,2,0,1:T(8,128)(2,1)S(1)}, u32[]{:S(2)}, u32[]{:S(2)}) collective-permute-start(bf16[2,3,16,256]{3,2,0,1:T(8,128)(2,1)S(1)} %pad_maximum_fusion.4), channel_id=1, source_target_pairs={{192,0},{200,8},{208,16},{216,24},{224,32},{232,40},{240,48},{248,... | collective-permute-start | bytes 147464 | tf_op jit(solution)/shard_map/ppermute | solution.py:32
  19.4 15.3 %collective-permute-start = (bf16[2,16,32,256]{3,1,2,0:T(8,128)(2,1)}, bf16[2,16,32,256]{3,1,2,0:T(8,128)(2,1)}, u32[]{:S(2)}, u32[]{:S(2)}) collective-permute-start(bf16[2,16,32,256]{3,1,2,0:T(8,128)(2,1)} %pad_maximum_fusion.2), channel_id=1, source_target_pairs={{64,0},{72,8},{80,16},{88,24},{96,32},{104,40},{112,48},{120,56},{... | collective-permute-start | bytes 1572872 | tf_op jit(solution)/shard_map/ppermute | solution.py:32
  20.9 13.8 %collective-permute-start.1 = (bf16[2,16,32,256]{3,1,2,0:T(8,128)(2,1)}, bf16[2,16,32,256]{3,1,2,0:T(8,128)(2,1)}, u32[]{:S(2)}, u32[]{:S(2)}) collective-permute-start(bf16[2,16,32,256]{3,1,2,0:T(8,128)(2,1)} %pad_maximum_fusion.2), channel_id=1, source_target_pairs={{128,0},{136,8},{144,16},{152,24},{160,32},{168,40},{176,48},{184,... | collective-permute-start | bytes 1572872 | tf_op jit(solution)/shard_map/ppermute | solution.py:32
  24.6 0.5 copy-start.10
  31.9 2.2 copy-start.15
  31.9 2.6 %copy-start.11 = (pred[16]{0:T(512)(128)(4,1)S(1)}, pred[16]{0:T(512)(128)(4,1)}, u32[]{:S(2)}) copy-start(pred[16]{0:T(512)(128)(4,1)} %get-tuple-element.66) | copy-start | bytes 52
  31.9 2.6 %copy-start.12 = (pred[16]{0:T(512)(128)(4,1)S(1)}, pred[16]{0:T(512)(128)(4,1)}, u32[]{:S(2)}) copy-start(pred[16]{0:T(512)(128)(4,1)} %get-tuple-element.67) | copy-start | bytes 52
  31.9 2.6 %copy-start.13 = (pred[16]{0:T(512)(128)(4,1)S(1)}, pred[16]{0:T(512)(128)(4,1)}, u32[]{:S(2)}) copy-start(pred[16]{0:T(512)(128)(4,1)} %get-tuple-element.68) | copy-start | bytes 52
  31.9 2.6 %copy-start.14 = (pred[16]{0:T(512)(128)(4,1)S(1)}, pred[16]{0:T(512)(128)(4,1)}, u32[]{:S(2)}) copy-start(pred[16]{0:T(512)(128)(4,1)} %get-tuple-element.69) | copy-start | bytes 52
  34.2 11.7 %collective-permute-start.2 = (bf16[2,16,32,256]{3,1,2,0:T(8,128)(2,1)}, bf16[2,16,32,256]{3,1,2,0:T(8,128)(2,1)S(1)}, u32[]{:S(2)}, u32[]{:S(2)}) collective-permute-start(bf16[2,16,32,256]{3,1,2,0:T(8,128)(2,1)} %pad_maximum_fusion.2), channel_id=1, source_target_pairs={{192,0},{200,8},{208,16},{216,24},{224,32},{232,40},{240,48},{248,... | collective-permute-start | bytes 1572872 | tf_op jit(solution)/shard_map/ppermute | solution.py:32
  47.5 1.2 copy-start.5
  47.5 1.8 copy-start.4
  50.1 81.4 %copy-start.1 = (bf16[3,16,4096]{2,1,0:T(8,128)(2,1)S(1)}, bf16[3,16,4096]{2,1,0:T(8,128)(2,1)}, u32[]{:S(2)}) copy-start(bf16[3,16,4096]{2,1,0:T(8,128)(2,1)} %param.18) | copy-start | bytes 1179652
  50.2 82.7 %copy-start.8 = (f32[4096]{0:T(1024)S(1)}, f32[4096]{0:T(1024)}, u32[]{:S(2)}) copy-start(f32[4096]{0:T(1024)} %param.26) | copy-start | bytes 49156
  51.5 113.2 %all-gather.5.cloned.1.call-start = ((), (), s32[]{:S(2)}) async-start(), calls=%async_computation.2 | async-start | bytes 4325376 | tf_op jit(solution)/shard_map/all_gather | solution.py:80
  52.1 133.9 %all-gather.3.cloned.1.call-start = ((), (), s32[]{:S(2)}) async-start(), calls=%async_computation.1 | async-start | bytes 7077888 | tf_op jit(solution)/shard_map/all_gather | solution.py:81
  131.6 2.6 %copy-start.3 = (bf16[4096,256]{1,0:T(8,128)(2,1)S(1)}, bf16[4096,256]{1,0:T(8,128)(2,1)}, u32[]{:S(2)}) copy-start(bf16[4096,256]{1,0:T(8,128)(2,1)} %param.27) | copy-start | bytes 6291460
  134.7 25.9 %collective-permute-start.9 = (bf16[3,4,256]{2,1,0:T(4,128)(2,1)S(1)}, bf16[3,4,256]{2,1,0:T(4,128)(2,1)S(1)}, u32[]{:S(2)}, u32[]{:S(2)}) collective-permute-start(bf16[3,4,256]{2,1,0:T(4,128)(2,1)S(1)} %get-tuple-element.43), channel_id=1, source_target_pairs={{0,24},{8,56},{16,88},{24,120},{32,152},{40,184},{48,216},{56,248}... | collective-permute-start | bytes 18440 | tf_op jit(solution)/shard_map/ppermute | solution.py:166
  139.3 21.3 %collective-permute-start.8 = (bf16[3,4,256]{2,1,0:T(4,128)(2,1)S(1)}, bf16[3,4,256]{2,1,0:T(4,128)(2,1)S(1)}, u32[]{:S(2)}, u32[]{:S(2)}) collective-permute-start(bf16[3,4,256]{2,1,0:T(4,128)(2,1)S(1)} %get-tuple-element.44), channel_id=1, source_target_pairs={{0,16},{8,48},{16,80},{24,112},{32,144},{40,176},{48,208},{56,240}... | collective-permute-start | bytes 18440 | tf_op jit(solution)/shard_map/ppermute | solution.py:166
  151.8 8.8 %collective-permute-start.7 = (bf16[3,4,256]{2,1,0:T(4,128)(2,1)S(1)}, bf16[3,4,256]{2,1,0:T(4,128)(2,1)S(1)}, u32[]{:S(2)}, u32[]{:S(2)}) collective-permute-start(bf16[3,4,256]{2,1,0:T(4,128)(2,1)S(1)} %get-tuple-element.45), channel_id=1, source_target_pairs={{0,8},{8,40},{16,72},{24,104},{32,136},{40,168},{48,200},{56,232},... | collective-permute-start | bytes 18440 | tf_op jit(solution)/shard_map/ppermute | solution.py:166
  157.3 7.4 %collective-permute-start.6 = (bf16[3,4,256]{2,1,0:T(4,128)(2,1)S(1)}, bf16[3,4,256]{2,1,0:T(4,128)(2,1)S(1)}, u32[]{:S(2)}, u32[]{:S(2)}) collective-permute-start(bf16[3,4,256]{2,1,0:T(4,128)(2,1)S(1)} %get-tuple-element.42), channel_id=1, source_target_pairs={{0,0},{8,32},{16,64},{24,96},{32,128},{40,160},{48,192},{56,224},{... | collective-permute-start | bytes 18440 | tf_op jit(solution)/shard_map/ppermute | solution.py:166
  194.3 16.3 %collective-permute-start.13 = (bf16[3,4,256]{2,1,0:T(4,128)(2,1)S(1)}, bf16[3,4,256]{2,1,0:T(4,128)(2,1)S(1)}, u32[]{:S(2)}, u32[]{:S(2)}) collective-permute-start(bf16[3,4,256]{2,1,0:T(4,128)(2,1)S(1)} %squeeze.124), channel_id=1, source_target_pairs={{24,0},{56,8},{88,16},{120,24},{152,32},{184,40},{216,48},{248,56}... | collective-permute-start | bytes 18440 | tf_op jit(solution)/shard_map/ppermute | solution.py:177
  199.9 10.7 %collective-permute-start.12 = (bf16[3,4,256]{2,1,0:T(4,128)(2,1)S(1)}, bf16[3,4,256]{2,1,0:T(4,128)(2,1)S(1)}, u32[]{:S(2)}, u32[]{:S(2)}) collective-permute-start(bf16[3,4,256]{2,1,0:T(4,128)(2,1)S(1)} %squeeze.123), channel_id=1, source_target_pairs={{16,0},{48,8},{80,16},{112,24},{144,32},{176,40},{208,48},{240,56}... | collective-permute-start | bytes 18440 | tf_op jit(solution)/shard_map/ppermute | solution.py:177
  201.7 8.9 %collective-permute-start.11 = (bf16[3,4,256]{2,1,0:T(4,128)(2,1)S(1)}, bf16[3,4,256]{2,1,0:T(4,128)(2,1)S(1)}, u32[]{:S(2)}, u32[]{:S(2)}) collective-permute-start(bf16[3,4,256]{2,1,0:T(4,128)(2,1)S(1)} %squeeze.122), channel_id=1, source_target_pairs={{8,0},{40,8},{72,16},{104,24},{136,32},{168,40},{200,48},{232,56},... | collective-permute-start | bytes 18440 | tf_op jit(solution)/shard_map/ppermute | solution.py:177
  207.6 8.6 %collective-permute-start.10 = (bf16[3,4,256]{2,1,0:T(4,128)(2,1)S(1)}, bf16[3,4,256]{2,1,0:T(4,128)(2,1)S(1)}, u32[]{:S(2)}, u32[]{:S(2)}) collective-permute-start(bf16[3,4,256]{2,1,0:T(4,128)(2,1)S(1)} %squeeze.121), channel_id=1, source_target_pairs={{0,0},{32,8},{64,16},{96,24},{128,32},{160,40},{192,48},{224,56},{... | collective-permute-start | bytes 18440 | tf_op jit(solution)/shard_map/ppermute | solution.py:177
Sparse Core Ops, SparseCore 0:
  51.6 79.8 all-reduce.1
Sparse Core Ops, SparseCore 1:
  54.5 55.5 all-gather.4
  111.8 74.1 all-gather.2
where the time goes:
time: 225 us
  waiting for transfers between devices  121 us (54%)
  starting transfers between devices  48.4 us (22%)
  between operations  16.9 us (8%)
  matrix products  16.7 us (7%)
  other arithmetic  13.6 us (6%)
  local copies, waits for them, and re-layouts  8.23 us (4%)
    psum x1, waiting for transfers between devices, shards(): lax.psum(partial_out.astype(jnp.bfloat16), 'head').astype(jnp.float32)  78.1 us
    ppermute x4, starting transfers between devices, shards(): sent.append(lax.ppermute(piece, 'hyp', route))  25.9 us
    all_gather x1, waiting for transfers between devices, shards(): full_rows = lax.all_gather(encoder_rows, 'head', axis=1, tiled=True)  21.2 us
    ppermute x4, starting transfers between devices, shards(): back.append(lax.ppermute(answer[shift], 'hyp', route))  16.2 us
    ppermute x6, waiting for transfers between devices, beam_copies(): copies.append(lax.ppermute(block, 'hyp', route))  11.1 us
    dot_general x1, matrix products, shards(): jnp.dot(full_rows, full_weights, preferred_element_type=jnp.float32)  7.47 us
    ppermute x6, starting transfers between devices, beam_copies(): copies.append(lax.ppermute(block, 'hyp', route))  6.19 us
    ppermute x4, waiting for transfers between devices, shards(): back.append(lax.ppermute(answer[shift], 'hyp', route))  5.57 us
  transfers between devices with their start and end apart: 17, of which 5 were waited for; matrix products, arithmetic and copies ran while one was open for 7% of the time, Pallas kernels for 0%

commit v1 on v0

--- a/solution.py
+++ b/solution.py
@@ -8,6 +8,19 @@
 TARGETS = 4
 STEPS = 3
 EPSILON = 1e-06
+
+
+def gather_around(shard, axis, dim):
+    ways = lax.axis_size(axis)
+    up = [(d, (d + 1) % ways) for d in range(ways)]
+    down = [(d, (d - 1) % ways) for d in range(ways)]
+    earlier, later = ([shard], [shard])
+    for _ in range(ways // 2):
+        earlier.append(lax.ppermute(earlier[-1], axis, up))
+    for _ in range((ways - 1) // 2):
+        later.append(lax.ppermute(later[-1], axis, down))
+    line = jnp.concatenate([*earlier[::-1], *later[1:]], axis=dim)
+    return jnp.roll(line, (lax.axis_index(axis) - ways // 2) * shard.shape[dim], axis=dim)
 
 
 def rms_scaled(values_in, gain):
@@ -78,7 +91,7 @@
     past_len = past_keys.shape[1]
     scaling = HEAD ** (-0.5)
     full_weights = lax.all_gather(cross_wkv, "hyp", axis=0, tiled=True)
-    full_rows = lax.all_gather(encoder_rows, "head", axis=1, tiled=True)
+    full_rows = gather_around(encoder_rows, "head", 1)
     cross_kv = jnp.dot(full_rows, full_weights, preferred_element_type=jnp.float32).astype(
         jnp.bfloat16
     )

time: 225 us -> 226 us (level)
  the two profiles are of different devices: /device:TPU:17 before, /device:TPU:14 now
where the time goes in v1:
time: 226 us; the launch traced here: 225 us
  waiting for transfers between devices  83.1 us (37%)
  starting transfers between devices  50.5 us (22%)
  local copies, waits for them, and re-layouts  38.7 us (17%)
  matrix products  19.9 us (9%)
  between operations  16.7 us (7%)
  other arithmetic  16 us (7%)
    ppermute x4, waiting for transfers between devices, gather_around(): earlier.append(lax.ppermute(earlier[-1], axis, up))  39.2 us
    unnamed x39, local copies, waits for them, and re-layouts  28.8 us
    psum x1, waiting for transfers between devices, shards(): lax.psum(partial_out.astype(jnp.bfloat16), 'head').astype(jnp.float32)  28.1 us
    ppermute x4, starting transfers between devices, shards(): back.append(lax.ppermute(answer[shift], 'hyp', route))  17.7 us
    ppermute x4, starting transfers between devices, shards(): sent.append(lax.ppermute(piece, 'hyp', route))  13.8 us
    ppermute x3, starting transfers between devices, gather_around(): later.append(lax.ppermute(later[-1], axis, down))  8.37 us
    dot_general x1, matrix products, shards(): jnp.dot(full_rows, full_weights, preferred_element_type=jnp.float32)  7.47 us
    ppermute x6, starting transfers between devices, beam_copies(): copies.append(lax.ppermute(block, 'hyp', route))  7.04 us
  transfers between devices with their start and end apart: 23, of which 8 were waited for; matrix products, arithmetic and copies ran while one was open for 25% of the time, Pallas kernels for 0%

profile of v1, /device:TPU:14, one launch (start us, length us, event | category | flops | bytes accessed | tf_op | source)
XLA Modules:
  0.0 224.9 jit_solution(6001965818877092859)
XLA Ops:
  8.1 1.5 copy_bitcast_fusion
  10.2 0.8 pad_maximum_fusion.2
  11.5 2.6 %collective-permute-start.1 = (bf16[2,16,32,256]{3,1,2,0:T(8,128)(2,1)}, bf16[2,16,32,256]{3,1,2,0:T(8,128)(2,1)}, u32[]{:S(2)}, u32[]{:S(2)}) collective-permute-start(bf16[2,16,32,256]{3,1,2,0:T(8,128)(2,1)} %pad_maximum_fusion.2), channel_id=1, source_target_pairs={{128,0},{136,8},{144,16},{152,24},{160,32},{168,40},{176,48},{184,... | collective-permute-start | bytes 1572872 | tf_op jit(solution)/shard_map/ppermute | solution.py:45
  14.1 1.9 collective-permute-start.2
  16.0 0.8 constant_dynamic-slice_fusion.3
  16.9 1.1 fusion.47
  18.0 1.2 multiply_reduce_fusion.1
  19.2 1.2 multiply_convert_fusion.1
  20.3 2.1 convolution_convert_fusion.4
  22.5 2.1 convolution_convert_fusion.3
  25.4 1.3 collective-permute-start.4
  26.7 0.7 reshape.452
  29.6 0.7 gather_fusion.5
  30.4 0.7 gather_fusion.1
  31.1 0.7 gather_fusion.6
  33.7 2.1 convolution_convert_fusion.5
  35.8 0.7 broadcast_compare_fusion.7
  36.5 2.4 %collective-permute-done.3 = bf16[2,3,16,256]{3,2,0,1:T(8,128)(2,1)} collective-permute-done((bf16[2,3,16,256]{3,2,0,1:T(8,128)(2,1)}, bf16[2,3,16,256]{3,2,0,1:T(8,128)(2,1)}, u32[]{:S(2)}, u32[]{:S(2)}) %collective-permute-start.3) | collective-permute-done | bytes 49184 | tf_op jit(solution)/shard_map/ppermute | solution.py:45
  39.5 0.8 fusion.71
  40.2 2.9 %collective-permute-done.5 = bf16[2,3,16,256]{3,2,0,1:T(8,128)(2,1)S(1)} collective-permute-done((bf16[2,3,16,256]{3,2,0,1:T(8,128)(2,1)}, bf16[2,3,16,256]{3,2,0,1:T(8,128)(2,1)S(1)}, u32[]{:S(2)}, u32[]{:S(2)}) %collective-permute-start.5) | collective-permute-done | bytes 49184 | tf_op jit(solution)/shard_map/ppermute | solution.py:45
  43.1 0.9 fusion.40
  44.0 0.8 fusion.37
  44.9 1.8 select_select_fusion.2
  49.6 1.2 convolution_convert_fusion
  51.4 2.0 collective-permute-start.10
  53.4 21.8 %collective-permute-done.10 = bf16[768,512]{1,0:T(8,128)(2,1)S(1)} collective-permute-done((bf16[768,512]{1,0:T(8,128)(2,1)S(1)}, bf16[768,512]{1,0:T(8,128)(2,1)S(1)}, u32[]{:S(2)}, u32[]{:S(2)}) %collective-permute-start.10) | collective-permute-done | bytes 786464 | tf_op jit(solution)/shard_map/ppermute | solution.py:19
  75.2 0.9 copy-done.3
  76.1 3.2 %collective-permute-start.14 = (bf16[768,512]{1,0:T(8,128)(2,1)S(1)}, bf16[768,512]{1,0:T(8,128)(2,1)}, u32[]{:S(2)}, u32[]{:S(2)}) collective-permute-start(bf16[768,512]{1,0:T(8,128)(2,1)S(1)} %copy-done.2), channel_id=1, source_target_pairs={{0,7},{1,0},{2,1},{3,2},{4,3},{5,4},{6,5},{7,6},{8,15},{9,8},{10,9... | collective-permute-start | bytes 2359304 | tf_op jit(solution)/shard_map/ppermute | solution.py:21
  79.4 17.4 %collective-permute-done.11 = bf16[768,512]{1,0:T(8,128)(2,1)} collective-permute-done((bf16[768,512]{1,0:T(8,128)(2,1)S(1)}, bf16[768,512]{1,0:T(8,128)(2,1)}, u32[]{:S(2)}, u32[]{:S(2)}) %collective-permute-start.11) | collective-permute-done | bytes 786464 | tf_op jit(solution)/shard_map/ppermute | solution.py:19
  97.3 3.2 %collective-permute-start.15 = (bf16[768,512]{1,0:T(8,128)(2,1)}, bf16[768,512]{1,0:T(8,128)(2,1)}, u32[]{:S(2)}, u32[]{:S(2)}) collective-permute-start(bf16[768,512]{1,0:T(8,128)(2,1)} %collective-permute-done.14), channel_id=1, source_target_pairs={{0,7},{1,0},{2,1},{3,2},{4,3},{5,4},{6,5},{7,6},{8,15},{9,8},{10,9... | collective-permute-start | bytes 2359304 | tf_op jit(solution)/shard_map/ppermute | solution.py:21
  100.6 28.1 %all-reduce.2.cloned.1.call-done = bf16[3,16,4096]{2,1,0:T(8,128)(2,1)} async-done(((bf16[3,16,4096]{2,1,0:T(8,128)(2,1)}), bf16[3,16,4096]{2,1,0:T(8,128)(2,1)}) %all-reduce.2.cloned.1.call-update) | async-done | bytes 393232 | tf_op jit(solution)/shard_map/psum | solution.py:164
  128.7 1.2 multiply_reduce_fusion
  129.9 1.5 collective-permute-start.13
  131.4 1.2 multiply_convert_fusion
  132.6 2.1 convolution_convert_fusion.2
  134.7 1.9 collective-permute-start.6
  137.9 4.8 %collective-permute-start.7 = (bf16[3,4,256]{2,1,0:T(4,128)(2,1)S(1)}, bf16[3,4,256]{2,1,0:T(4,128)(2,1)S(1)}, u32[]{:S(2)}, u32[]{:S(2)}) collective-permute-start(bf16[3,4,256]{2,1,0:T(4,128)(2,1)S(1)} %get-tuple-element.45), channel_id=1, source_target_pairs={{0,8},{8,40},{16,72},{24,104},{32,136},{40,168},{48,200},{56,232},... | collective-permute-start | bytes 18440 | tf_op jit(solution)/shard_map/ppermute | solution.py:179
  142.8 2.2 collective-permute-start.8
  145.0 4.8 %collective-permute-start.9 = (bf16[3,4,256]{2,1,0:T(4,128)(2,1)S(1)}, bf16[3,4,256]{2,1,0:T(4,128)(2,1)S(1)}, u32[]{:S(2)}, u32[]{:S(2)}) collective-permute-start(bf16[3,4,256]{2,1,0:T(4,128)(2,1)S(1)} %get-tuple-element.43), channel_id=1, source_target_pairs={{0,24},{8,56},{16,88},{24,120},{32,152},{40,184},{48,216},{56,248}... | collective-permute-start | bytes 18440 | tf_op jit(solution)/shard_map/ppermute | solution.py:179
  149.8 4.0 %collective-permute-done.9 = bf16[3,4,256]{2,1,0:T(4,128)(2,1)S(1)} collective-permute-done((bf16[3,4,256]{2,1,0:T(4,128)(2,1)S(1)}, bf16[3,4,256]{2,1,0:T(4,128)(2,1)S(1)}, u32[]{:S(2)}, u32[]{:S(2)}) %collective-permute-start.9) | collective-permute-done | bytes 6176 | tf_op jit(solution)/shard_map/ppermute | solution.py:179
  153.9 1.9 collective-permute-start.16
  155.8 2.2 constant_dynamic-update-slice_fusion.15
  158.0 2.1 constant_dynamic-update-slice_fusion.14
  160.1 2.1 constant_dynamic-update-slice_fusion.13
  162.2 2.1 constant_dynamic-update-slice_fusion.12
  164.3 1.0 constant_dynamic-update-slice_fusion.11
  165.2 2.1 constant_dynamic-update-slice_fusion.10
  167.3 2.1 constant_dynamic-update-slice_fusion.9
  169.4 1.3 collective-permute-done.16
  170.8 0.9 constant_dynamic-update-slice_fusion.8
  171.7 2.1 constant_dynamic-update-slice_fusion.7
  173.8 2.2 constant_dynamic-update-slice_fusion.6
  176.0 2.1 constant_dynamic-update-slice_fusion.5
  178.1 1.0 constant_dynamic-update-slice_fusion.4
  179.1 1.0 constant_dynamic-update-slice_fusion.3
  180.1 2.1 constant_dynamic-update-slice_fusion.2
  182.2 2.1 constant_dynamic-update-slice_fusion.1
  184.3 1.0 constant_dynamic-update-slice_fusion
  185.3 7.5 %fusion.2 = bf16[768,512]{0,1:T(8,128)(2,1)S(1)} fusion(bf16[4096,512]{1,0:T(8,128)(2,1)} %all-gather.2.cloned.1.call-done, bf16[768,8192]{1,0:T(8,128)(2,1)} %constant_dynamic-update-slice_fusion, s32[]{:T(128)S(6)} %select_n.355), kind=kOutput, calls=%fused_computation.10 | convolution fusion | flops 3221618688 | bytes 11272196 | tf_op jit(solution)/shard_map/dot_general | solution.py:95
  193.6 2.3 %collective-permute-start.17 = (bf16[3,4,256]{2,1,0:T(4,128)(2,1)S(1)}, bf16[3,4,256]{2,1,0:T(4,128)(2,1)S(1)}, u32[]{:S(2)}, u32[]{:S(2)}) collective-permute-start(bf16[3,4,256]{2,1,0:T(4,128)(2,1)S(1)} %squeeze.121), channel_id=1, source_target_pairs={{0,0},{32,8},{64,16},{96,24},{128,32},{160,40},{192,48},{224,56},{... | collective-permute-start | bytes 18440 | tf_op jit(solution)/shard_map/ppermute | solution.py:190
  196.0 7.8 %collective-permute-start.18 = (bf16[3,4,256]{2,1,0:T(4,128)(2,1)S(1)}, bf16[3,4,256]{2,1,0:T(4,128)(2,1)S(1)}, u32[]{:S(2)}, u32[]{:S(2)}) collective-permute-start(bf16[3,4,256]{2,1,0:T(4,128)(2,1)S(1)} %squeeze.122), channel_id=1, source_target_pairs={{8,0},{40,8},{72,16},{104,24},{136,32},{168,40},{200,48},{232,56},... | collective-permute-start | bytes 18440 | tf_op jit(solution)/shard_map/ppermute | solution.py:190
  203.8 3.2 %collective-permute-start.19 = (bf16[3,4,256]{2,1,0:T(4,128)(2,1)S(1)}, bf16[3,4,256]{2,1,0:T(4,128)(2,1)S(1)}, u32[]{:S(2)}, u32[]{:S(2)}) collective-permute-start(bf16[3,4,256]{2,1,0:T(4,128)(2,1)S(1)} %squeeze.123), channel_id=1, source_target_pairs={{16,0},{48,8},{80,16},{112,24},{144,32},{176,40},{208,48},{240,56}... | collective-permute-start | bytes 18440 | tf_op jit(solution)/shard_map/ppermute | solution.py:190
  207.0 4.4 %collective-permute-start.20 = (bf16[3,4,256]{2,1,0:T(4,128)(2,1)S(1)}, bf16[3,4,256]{2,1,0:T(4,128)(2,1)S(1)}, u32[]{:S(2)}, u32[]{:S(2)}) collective-permute-start(bf16[3,4,256]{2,1,0:T(4,128)(2,1)S(1)} %squeeze.124), channel_id=1, source_target_pairs={{24,0},{56,8},{88,16},{120,24},{152,32},{184,40},{216,48},{248,56}... | collective-permute-start | bytes 18440 | tf_op jit(solution)/shard_map/ppermute | solution.py:190
  211.5 4.6 %collective-permute-done.20 = bf16[3,4,256]{2,1,0:T(4,128)(2,1)S(1)} collective-permute-done((bf16[3,4,256]{2,1,0:T(4,128)(2,1)S(1)}, bf16[3,4,256]{2,1,0:T(4,128)(2,1)S(1)}, u32[]{:S(2)}, u32[]{:S(2)}) %collective-permute-start.20) | collective-permute-done | bytes 6176 | tf_op jit(solution)/shard_map/ppermute | solution.py:190
  (119 shorter events, 13.9 us)
Async XLA Ops:
  8.0 41.6 %copy-start = (bf16[256,4096]{1,0:T(8,128)(2,1)S(1)}, bf16[256,4096]{1,0:T(8,128)(2,1)}, u32[]{:S(2)}) copy-start(bf16[256,4096]{1,0:T(8,128)(2,1)} %param.25) | copy-start | bytes 6291460
  8.0 120.6 %all-reduce.2.cloned.1.call-start = ((), (), s32[]{:S(2)}) async-start(), calls=%async_computation | async-start | bytes 786432 | tf_op jit(solution)/shard_map/psum | solution.py:164
  9.5 0.7 copy-start.5
  9.5 1.5 copy-start.6
  11.1 33.8 %collective-permute-start = (bf16[2,16,32,256]{3,1,2,0:T(8,128)(2,1)}, bf16[2,16,32,256]{3,1,2,0:T(8,128)(2,1)}, u32[]{:S(2)}, u32[]{:S(2)}) collective-permute-start(bf16[2,16,32,256]{3,1,2,0:T(8,128)(2,1)} %pad_maximum_fusion.2), channel_id=1, source_target_pairs={{64,0},{72,8},{80,16},{88,24},{96,32},{104,40},{112,48},{120,56},{... | collective-permute-start | bytes 1572872 | tf_op jit(solution)/shard_map/ppermute | solution.py:45
  11.5 33.4 %collective-permute-start.1 = (bf16[2,16,32,256]{3,1,2,0:T(8,128)(2,1)}, bf16[2,16,32,256]{3,1,2,0:T(8,128)(2,1)}, u32[]{:S(2)}, u32[]{:S(2)}) collective-permute-start(bf16[2,16,32,256]{3,1,2,0:T(8,128)(2,1)} %pad_maximum_fusion.2), channel_id=1, source_target_pairs={{128,0},{136,8},{144,16},{152,24},{160,32},{168,40},{176,48},{184,... | collective-permute-start | bytes 1572872 | tf_op jit(solution)/shard_map/ppermute | solution.py:45
  14.1 30.8 %collective-permute-start.2 = (bf16[2,16,32,256]{3,1,2,0:T(8,128)(2,1)}, bf16[2,16,32,256]{3,1,2,0:T(8,128)(2,1)}, u32[]{:S(2)}, u32[]{:S(2)}) collective-permute-start(bf16[2,16,32,256]{3,1,2,0:T(8,128)(2,1)} %pad_maximum_fusion.2), channel_id=1, source_target_pairs={{192,0},{200,8},{208,16},{216,24},{224,32},{232,40},{240,48},{248,... | collective-permute-start | bytes 1572872 | tf_op jit(solution)/shard_map/ppermute | solution.py:45
  22.4 2.2 copy-start.8
  22.4 106.2 %copy-start.1 = (bf16[3,16,4096]{2,1,0:T(8,128)(2,1)S(1)}, bf16[3,16,4096]{2,1,0:T(8,128)(2,1)}, u32[]{:S(2)}) copy-start(bf16[3,16,4096]{2,1,0:T(8,128)(2,1)} %param.18) | copy-start | bytes 1179652
  22.4 108.9 %copy-start.11 = (f32[4096]{0:T(1024)S(1)}, f32[4096]{0:T(1024)}, u32[]{:S(2)}) copy-start(f32[4096]{0:T(1024)} %param.26) | copy-start | bytes 49156
  24.6 0.6 copy-start.9
  25.2 13.6 %collective-permute-start.3 = (bf16[2,3,16,256]{3,2,0,1:T(8,128)(2,1)}, bf16[2,3,16,256]{3,2,0,1:T(8,128)(2,1)}, u32[]{:S(2)}, u32[]{:S(2)}) collective-permute-start(bf16[2,3,16,256]{3,2,0,1:T(8,128)(2,1)} %pad_maximum_fusion.4), channel_id=1, source_target_pairs={{64,0},{72,8},{80,16},{88,24},{96,32},{104,40},{112,48},{120,56},{... | collective-permute-start | bytes 147464 | tf_op jit(solution)/shard_map/ppermute | solution.py:45
  25.4 14.9 %collective-permute-start.4 = (bf16[2,3,16,256]{3,2,0,1:T(8,128)(2,1)}, bf16[2,3,16,256]{3,2,0,1:T(8,128)(2,1)}, u32[]{:S(2)}, u32[]{:S(2)}) collective-permute-start(bf16[2,3,16,256]{3,2,0,1:T(8,128)(2,1)} %pad_maximum_fusion.4), channel_id=1, source_target_pairs={{128,0},{136,8},{144,16},{152,24},{160,32},{168,40},{176,48},{184,... | collective-permute-start | bytes 147464 | tf_op jit(solution)/shard_map/ppermute | solution.py:45
  35.7 15.7 %copy-start.2 = (bf16[768,512]{1,0:T(8,128)(2,1)S(1)}, bf16[768,512]{1,0:T(8,128)(2,1)}, u32[]{:S(2)}) copy-start(bf16[768,512]{1,0:T(8,128)(2,1)} %param.29) | copy-start | bytes 2359300
  38.8 4.3 %collective-permute-start.5 = (bf16[2,3,16,256]{3,2,0,1:T(8,128)(2,1)}, bf16[2,3,16,256]{3,2,0,1:T(8,128)(2,1)S(1)}, u32[]{:S(2)}, u32[]{:S(2)}) collective-permute-start(bf16[2,3,16,256]{3,2,0,1:T(8,128)(2,1)} %pad_maximum_fusion.4), channel_id=1, source_target_pairs={{192,0},{200,8},{208,16},{216,24},{224,32},{232,40},{240,48},{248,... | collective-permute-start | bytes 147464 | tf_op jit(solution)/shard_map/ppermute | solution.py:45
  48.1 1.2 copy-start.7
  48.1 1.4 copy-start.10
  50.9 134.4 %all-gather.2.cloned.1.call-start = ((), (), s32[]{:S(2)}) async-start(), calls=%async_computation.1 | async-start | bytes 4325376 | tf_op jit(solution)/shard_map/all_gather | solution.py:93
  51.4 23.8 %collective-permute-start.10 = (bf16[768,512]{1,0:T(8,128)(2,1)S(1)}, bf16[768,512]{1,0:T(8,128)(2,1)S(1)}, u32[]{:S(2)}, u32[]{:S(2)}) collective-permute-start(bf16[768,512]{1,0:T(8,128)(2,1)S(1)} %copy-done.2), channel_id=1, source_target_pairs={{0,1},{1,2},{2,3},{3,4},{4,5},{5,6},{6,7},{7,0},{8,9},{9,10},{10,1... | collective-permute-start | bytes 2359304 | tf_op jit(solution)/shard_map/ppermute | solution.py:19
  75.2 0.9 copy-start.3
  76.1 20.7 %collective-permute-start.11 = (bf16[768,512]{1,0:T(8,128)(2,1)S(1)}, bf16[768,512]{1,0:T(8,128)(2,1)}, u32[]{:S(2)}, u32[]{:S(2)}) collective-permute-start(bf16[768,512]{1,0:T(8,128)(2,1)S(1)} %collective-permute-done.10), channel_id=1, source_target_pairs={{0,1},{1,2},{2,3},{3,4},{4,5},{5,6},{6,7},{7,0},{8,9},{9,10},{10,1... | collective-permute-start | bytes 2359304 | tf_op jit(solution)/shard_map/ppermute | solution.py:19
  76.1 21.2 %collective-permute-start.14 = (bf16[768,512]{1,0:T(8,128)(2,1)S(1)}, bf16[768,512]{1,0:T(8,128)(2,1)}, u32[]{:S(2)}, u32[]{:S(2)}) collective-permute-start(bf16[768,512]{1,0:T(8,128)(2,1)S(1)} %copy-done.2), channel_id=1, source_target_pairs={{0,7},{1,0},{2,1},{3,2},{4,3},{5,4},{6,5},{7,6},{8,15},{9,8},{10,9... | collective-permute-start | bytes 2359304 | tf_op jit(solution)/shard_map/ppermute | solution.py:21
  96.8 33.1 %collective-permute-start.12 = (bf16[768,512]{1,0:T(8,128)(2,1)}, bf16[768,512]{1,0:T(8,128)(2,1)}, u32[]{:S(2)}, u32[]{:S(2)}) collective-permute-start(bf16[768,512]{1,0:T(8,128)(2,1)} %collective-permute-done.11), channel_id=1, source_target_pairs={{0,1},{1,2},{2,3},{3,4},{4,5},{5,6},{6,7},{7,0},{8,9},{9,10},{10,1... | collective-permute-start | bytes 2359304 | tf_op jit(solution)/shard_map/ppermute | solution.py:19
  97.3 56.5 %collective-permute-start.15 = (bf16[768,512]{1,0:T(8,128)(2,1)}, bf16[768,512]{1,0:T(8,128)(2,1)}, u32[]{:S(2)}, u32[]{:S(2)}) collective-permute-start(bf16[768,512]{1,0:T(8,128)(2,1)} %collective-permute-done.14), channel_id=1, source_target_pairs={{0,7},{1,0},{2,1},{3,2},{4,3},{5,4},{6,5},{7,6},{8,15},{9,8},{10,9... | collective-permute-start | bytes 2359304 | tf_op jit(solution)/shard_map/ppermute | solution.py:21
  129.9 25.9 %collective-permute-start.13 = (bf16[768,512]{1,0:T(8,128)(2,1)}, bf16[768,512]{1,0:T(8,128)(2,1)}, u32[]{:S(2)}, u32[]{:S(2)}) collective-permute-start(bf16[768,512]{1,0:T(8,128)(2,1)} %collective-permute-done.12), channel_id=1, source_target_pairs={{0,1},{1,2},{2,3},{3,4},{4,5},{5,6},{6,7},{7,0},{8,9},{9,10},{10,1... | collective-permute-start | bytes 2359304 | tf_op jit(solution)/shard_map/ppermute | solution.py:19
  134.7 10.3 %collective-permute-start.6 = (bf16[3,4,256]{2,1,0:T(4,128)(2,1)S(1)}, bf16[3,4,256]{2,1,0:T(4,128)(2,1)S(1)}, u32[]{:S(2)}, u32[]{:S(2)}) collective-permute-start(bf16[3,4,256]{2,1,0:T(4,128)(2,1)S(1)} %get-tuple-element.42), channel_id=1, source_target_pairs={{0,0},{8,32},{16,64},{24,96},{32,128},{40,160},{48,192},{56,224},{... | collective-permute-start | bytes 18440 | tf_op jit(solution)/shard_map/ppermute | solution.py:179
  137.9 11.9 %collective-permute-start.7 = (bf16[3,4,256]{2,1,0:T(4,128)(2,1)S(1)}, bf16[3,4,256]{2,1,0:T(4,128)(2,1)S(1)}, u32[]{:S(2)}, u32[]{:S(2)}) collective-permute-start(bf16[3,4,256]{2,1,0:T(4,128)(2,1)S(1)} %get-tuple-element.45), channel_id=1, source_target_pairs={{0,8},{8,40},{16,72},{24,104},{32,136},{40,168},{48,200},{56,232},... | collective-permute-start | bytes 18440 | tf_op jit(solution)/shard_map/ppermute | solution.py:179
  142.8 7.1 %collective-permute-start.8 = (bf16[3,4,256]{2,1,0:T(4,128)(2,1)S(1)}, bf16[3,4,256]{2,1,0:T(4,128)(2,1)S(1)}, u32[]{:S(2)}, u32[]{:S(2)}) collective-permute-start(bf16[3,4,256]{2,1,0:T(4,128)(2,1)S(1)} %get-tuple-element.44), channel_id=1, source_target_pairs={{0,16},{8,48},{16,80},{24,112},{32,144},{40,176},{48,208},{56,240}... | collective-permute-start | bytes 18440 | tf_op jit(solution)/shard_map/ppermute | solution.py:179
  145.0 8.8 %collective-permute-start.9 = (bf16[3,4,256]{2,1,0:T(4,128)(2,1)S(1)}, bf16[3,4,256]{2,1,0:T(4,128)(2,1)S(1)}, u32[]{:S(2)}, u32[]{:S(2)}) collective-permute-start(bf16[3,4,256]{2,1,0:T(4,128)(2,1)S(1)} %get-tuple-element.43), channel_id=1, source_target_pairs={{0,24},{8,56},{16,88},{24,120},{32,152},{40,184},{48,216},{56,248}... | collective-permute-start | bytes 18440 | tf_op jit(solution)/shard_map/ppermute | solution.py:179
  153.9 24.2 %copy-start.4 = (bf16[768,512]{1,0:T(8,128)(2,1)S(1)}, bf16[768,512]{1,0:T(8,128)(2,1)}, u32[]{:S(2)}) copy-start(bf16[768,512]{1,0:T(8,128)(2,1)} %copy-done.3) | copy-start | bytes 2359300
  153.9 16.9 %collective-permute-start.16 = (bf16[768,512]{1,0:T(8,128)(2,1)}, bf16[768,512]{1,0:T(8,128)(2,1)S(1)}, u32[]{:S(2)}, u32[]{:S(2)}) collective-permute-start(bf16[768,512]{1,0:T(8,128)(2,1)} %collective-permute-done.15), channel_id=1, source_target_pairs={{0,7},{1,0},{2,1},{3,2},{4,3},{5,4},{6,5},{7,6},{8,15},{9,8},{10,9... | collective-permute-start | bytes 2359304 | tf_op jit(solution)/shard_map/ppermute | solution.py:21
  193.6 17.8 %collective-permute-start.17 = (bf16[3,4,256]{2,1,0:T(4,128)(2,1)S(1)}, bf16[3,4,256]{2,1,0:T(4,128)(2,1)S(1)}, u32[]{:S(2)}, u32[]{:S(2)}) collective-permute-start(bf16[3,4,256]{2,1,0:T(4,128)(2,1)S(1)} %squeeze.121), channel_id=1, source_target_pairs={{0,0},{32,8},{64,16},{96,24},{128,32},{160,40},{192,48},{224,56},{... | collective-permute-start | bytes 18440 | tf_op jit(solution)/shard_map/ppermute | solution.py:190
  196.0 15.5 %collective-permute-start.18 = (bf16[3,4,256]{2,1,0:T(4,128)(2,1)S(1)}, bf16[3,4,256]{2,1,0:T(4,128)(2,1)S(1)}, u32[]{:S(2)}, u32[]{:S(2)}) collective-permute-start(bf16[3,4,256]{2,1,0:T(4,128)(2,1)S(1)} %squeeze.122), channel_id=1, source_target_pairs={{8,0},{40,8},{72,16},{104,24},{136,32},{168,40},{200,48},{232,56},... | collective-permute-start | bytes 18440 | tf_op jit(solution)/shard_map/ppermute | solution.py:190
  203.8 7.7 %collective-permute-start.19 = (bf16[3,4,256]{2,1,0:T(4,128)(2,1)S(1)}, bf16[3,4,256]{2,1,0:T(4,128)(2,1)S(1)}, u32[]{:S(2)}, u32[]{:S(2)}) collective-permute-start(bf16[3,4,256]{2,1,0:T(4,128)(2,1)S(1)} %squeeze.123), channel_id=1, source_target_pairs={{16,0},{48,8},{80,16},{112,24},{144,32},{176,40},{208,48},{240,56}... | collective-permute-start | bytes 18440 | tf_op jit(solution)/shard_map/ppermute | solution.py:190
  207.0 9.1 %collective-permute-start.20 = (bf16[3,4,256]{2,1,0:T(4,128)(2,1)S(1)}, bf16[3,4,256]{2,1,0:T(4,128)(2,1)S(1)}, u32[]{:S(2)}, u32[]{:S(2)}) collective-permute-start(bf16[3,4,256]{2,1,0:T(4,128)(2,1)S(1)} %squeeze.124), channel_id=1, source_target_pairs={{24,0},{56,8},{88,16},{120,24},{152,32},{184,40},{216,48},{248,56}... | collective-permute-start | bytes 18440 | tf_op jit(solution)/shard_map/ppermute | solution.py:190
Sparse Core Ops, SparseCore 0:
  51.0 77.6 all-reduce.1
Sparse Core Ops, SparseCore 1:
  53.9 52.4 all-gather.1
